TPU v7x, 128 devices: a whole 4x4x4 slice. The times are simulated.
128 devices in a mesh: grp: 4 (over x), tok: 32 (over z, y, core).
Axes of the slice: x: 4, y: 4, z: 4, core: 2. Of those that a mesh axis runs over, the one named last changes fastest.
Arguments:
- tokens: bfloat16 [16384, 2560], P(('grp', 'tok')), may hold values from -6 to 6
- input_gain: bfloat16 [2560], replicated, may hold values from 0.25 to 1.75
- query_down: bfloat16 [2560, 768], replicated, may hold values from -0.125 to 0.125
- query_gain: bfloat16 [768], replicated, may hold values from 0.25 to 1.75
- query_up: bfloat16 [768, 1920], replicated, may hold values from -0.21875 to 0.21875
- latent_down: bfloat16 [2560, 288], replicated, may hold values from -0.125 to 0.125
- latent_gain: bfloat16 [256], replicated, may hold values from 0.25 to 1.75
- key_up: bfloat16 [256, 1280], replicated, may hold values from -0.375 to 0.375
- value_up: bfloat16 [256, 1280], replicated, may hold values from -0.375 to 0.375
- output_weight: bfloat16 [1280, 2560], replicated, may hold values from -0.15625 to 0.15625
- post_gain: bfloat16 [2560], replicated, may hold values from 0.25 to 1.75
- gate_weight: bfloat16 [2560, 3200], P('tok', 'grp'), may hold values from -0.125 to 0.125
- up_weight: bfloat16 [2560, 3200], P('tok', 'grp'), may hold values from -0.125 to 0.125
- down_weight: bfloat16 [3200, 2560], P('grp', 'tok'), may hold values from -0.109375 to 0.109375
- cache_latents: bfloat16 [16, 4096, 288], P('grp', 'tok'), as said below
- prompt_latents: bfloat16 [8, 1024, 288], P(None, 'tok'), as said below
- cache_len: int32 [16], replicated, may hold values from 1 to 4096, 32768 in all
- prompt_len: int32 [8], replicated, may hold values from 1 to 1024, 4096 in all
- prompt_of: int32 [16], replicated, may hold values from 0 to 7
Outputs:
- layer_out: bfloat16 [16384, 2560], P(('grp', 'tok'))
- new_latents: bfloat16 [16384, 288], P(('grp', 'tok'))
Inputs may be any that keep to these rules, and one draw needn't show every extreme that they name: `cache_len`: some request has exactly 4096 live cached rows. `prompt_len`: some stored prompt has exactly 1024 live rows. `cache_latents`: rows past a request's live length are stored but never read. `prompt_latents`: rows past a prompt's live length are stored but never read.
All inputs are finite; a program needn't handle non-finite values.
Results may differ from a plain program's by a relative error of at most 0.02.
Values may be sent and summed in bfloat16 or wider, within the bound.
No kernel may reach another device: no remote copies, remote signals or barrier semaphores. Data moves between devices by JAX's collectives and lax.ppermute only.
A program may use at most 128 MiB of HBM per device.

v0:
```python
import jax
import jax.numpy as jnp
from jax import lax
from jax.sharding import PartitionSpec as P

KVR = 256
HEADS = 20
NOPE = 64
ROPE = 32
VDIM = 64
SPAN = 1024
EPSILON = 1e-06


def passed_along(block, axis, distance):
    devices = range(lax.axis_size(axis))
    route = [(i - distance, i) for i in devices if i - distance in devices]
    return lax.ppermute(block, axis, route)


def norm_rows(values, gain_vector):
    mean_square = jnp.mean(values * values, axis=-1, keepdims=True)
    return values * lax.rsqrt(mean_square + EPSILON) * gain_vector.astype(jnp.float32)


def rotate(values, positions):
    half_width = values.shape[-1] // 2
    frequency = 10000.0 ** (-jnp.arange(half_width, dtype=jnp.float32) / half_width)
    angles = positions.astype(jnp.float32)[:, None] * frequency[None, :]
    if values.ndim == 3:
        angles = angles[:, None, :]
    cosine = jnp.cos(angles)
    sine_part = jnp.sin(angles)
    leading = values[..., :half_width]
    trailing = values[..., half_width:]
    return jnp.concatenate(
        [leading * cosine - trailing * sine_part, trailing * cosine + leading * sine_part], axis=-1
    )


def attend_segment(
    softmax_state, queries, key_rows, lowers, limits, block_count, key_block, score_scale
):

    def fold_block(step_index, carried):
        running_max, running_sum, running_out = carried
        first_key = step_index * key_block
        key_piece = lax.dynamic_slice_in_dim(key_rows, first_key, key_block, 0)
        scores = (
            jnp.einsum("rw,kw->rk", queries, key_piece, preferred_element_type=jnp.float32)
            * score_scale
        )
        key_place = (first_key + jnp.arange(key_block, dtype=jnp.int32))[None, :]
        live_keys = jnp.logical_and(key_place >= lowers[:, None], key_place < limits[:, None])
        next_max = jnp.maximum(running_max, jnp.max(jnp.where(live_keys, scores, -1e30), axis=1))
        weights = jnp.where(live_keys, jnp.exp(scores - next_max[:, None]), 0.0)
        factor = jnp.exp(running_max - next_max)
        running_sum = running_sum * factor + jnp.sum(weights, axis=1)
        running_out = running_out * factor[:, None] + jnp.dot(
            weights.astype(jnp.bfloat16), key_piece[:, :KVR], preferred_element_type=jnp.float32
        )
        return (next_max, running_sum, running_out)

    return lax.fori_loop(0, block_count, fold_block, softmax_state)


def body(
    tokens,
    input_gain,
    query_down,
    query_gain,
    query_up,
    latent_down,
    latent_gain,
    key_up,
    value_up,
    output_weight,
    post_gain,
    gate_weight,
    up_weight,
    down_weight,
    cache_latents,
    prompt_latents,
    cache_len,
    prompt_len,
    prompt_of,
):
    group_index = lax.axis_index("grp")
    shard_index = lax.axis_index("tok")
    tok_dev = tokens.shape[0]
    tok_count = lax.axis_size("tok")
    group_requests = tok_dev * tok_count // SPAN
    local_request = shard_index % group_requests
    owner = group_index * group_requests + local_request
    offset = shard_index // group_requests * tok_dev
    within = offset + jnp.arange(tok_dev, dtype=jnp.int32)
    own_prompt = prompt_of[owner]
    prompt_live = prompt_len[own_prompt]
    cache_live = cache_len[owner]
    positions = prompt_live + cache_live + within
    normed = norm_rows(tokens.astype(jnp.float32), input_gain).astype(jnp.bfloat16)
    query_latent = norm_rows(
        jnp.dot(normed, query_down, preferred_element_type=jnp.float32), query_gain
    ).astype(jnp.bfloat16)
    query_full = jnp.dot(query_latent, query_up, preferred_element_type=jnp.float32).astype(
        jnp.bfloat16
    )
    query_full = lax.optimization_barrier(query_full).reshape(tok_dev, HEADS, NOPE + ROPE)
    absorbed = jnp.einsum(
        "thd,khd->thk",
        query_full[..., :NOPE],
        key_up.reshape(KVR, HEADS, NOPE),
        preferred_element_type=jnp.float32,
    )
    turned = rotate(query_full[..., NOPE:].astype(jnp.float32), positions)
    queries = jnp.concatenate([absorbed, turned], axis=-1).astype(jnp.bfloat16)
    latent_raw = jnp.dot(normed, latent_down, preferred_element_type=jnp.float32)
    new_latents = jnp.concatenate(
        [norm_rows(latent_raw[:, :KVR], latent_gain), rotate(latent_raw[:, KVR:], positions)],
        axis=-1,
    ).astype(jnp.bfloat16)
    latent_width = new_latents.shape[1]
    shards_back = SPAN // tok_dev
    earlier_pieces = []
    passing = new_latents
    for back in range(1, shards_back):
        passing = passed_along(passing, "tok", group_requests)
        earlier_pieces.insert(0, passing)
    span_rows = jnp.concatenate(earlier_pieces + [new_latents], axis=0)
    lead_rows = (shards_back - 1) * tok_dev
    span_lower = jnp.broadcast_to(lead_rows - offset, (tok_dev,))
    span_limit = lead_rows + 1 + jnp.arange(tok_dev, dtype=jnp.int32)
    cache_all, prompt_all = (
        lax.all_gather(cache_latents, "tok", axis=1, tiled=True),
        lax.all_gather(prompt_latents, "tok", axis=1, tiled=True),
    )
    cache_rows = lax.dynamic_index_in_dim(cache_all, local_request, 0, keepdims=False)
    prompt_rows = lax.dynamic_index_in_dim(prompt_all, own_prompt, 0, keepdims=False)
    query_rows = queries.reshape(tok_dev * HEADS, latent_width)
    row_count = tok_dev * HEADS
    score_scale = 1.0 / (NOPE + ROPE) ** 0.5
    softmax_state = (
        jnp.full((row_count,), -1e30, jnp.float32),
        jnp.zeros((row_count,), jnp.float32),
        jnp.zeros((row_count, KVR), jnp.float32),
    )
    no_lower = jnp.zeros((tok_dev,), jnp.int32)
    segments = (
        (prompt_rows, no_lower, jnp.broadcast_to(prompt_live, (tok_dev,))),
        (cache_rows, no_lower, jnp.broadcast_to(cache_live, (tok_dev,))),
        (span_rows, span_lower, span_limit),
    )
    for key_rows, token_lower, token_limit in segments:
        lowers = jnp.repeat(token_lower, HEADS)
        limits = jnp.repeat(token_limit, HEADS)
        key_block = min(512, key_rows.shape[0])
        block_count = key_rows.shape[0] // key_block
        softmax_state = attend_segment(
            softmax_state, query_rows, key_rows, lowers, limits, block_count, key_block, score_scale
        )
    running_max, running_sum, running_out = softmax_state
    latent_out = (
        (running_out / running_sum[:, None]).astype(jnp.bfloat16).reshape(tok_dev, HEADS, KVR)
    )
    heads_out = (
        jnp.einsum(
            "thk,khv->thv",
            latent_out,
            value_up.reshape(KVR, HEADS, VDIM),
            preferred_element_type=jnp.float32,
        )
        .astype(jnp.bfloat16)
        .reshape(tok_dev, HEADS * VDIM)
    )
    attended = jnp.dot(heads_out, output_weight, preferred_element_type=jnp.float32)
    residual = lax.optimization_barrier(
        (tokens.astype(jnp.float32) + attended).astype(jnp.bfloat16)
    )
    post_norm = norm_rows(residual.astype(jnp.float32), post_gain).astype(jnp.bfloat16)
    rows_all = lax.all_gather(post_norm, "grp", axis=0, tiled=True)
    gate_values = jnp.dot(
        rows_all,
        lax.all_gather(gate_weight, "tok", axis=0, tiled=True),
        preferred_element_type=jnp.float32,
    )
    up_values = jnp.dot(
        rows_all,
        lax.all_gather(up_weight, "tok", axis=0, tiled=True),
        preferred_element_type=jnp.float32,
    )
    hidden = (jax.nn.silu(gate_values) * up_values).astype(jnp.bfloat16)
    partial_out = jnp.dot(
        hidden,
        lax.all_gather(down_weight, "tok", axis=1, tiled=True),
        preferred_element_type=jnp.float32,
    )
    down_values = lax.psum_scatter(
        partial_out.astype(jnp.bfloat16), "grp", scatter_dimension=0, tiled=True
    ).astype(jnp.float32)
    layer_out = (residual.astype(jnp.float32) + down_values).astype(jnp.bfloat16)
    return (layer_out, new_latents)


def solution(mesh):
    in_specs = (
        P(("grp", "tok"), None),
        P(),
        P(),
        P(),
        P(),
        P(),
        P(),
        P(),
        P(),
        P(),
        P(),
        P("tok", "grp"),
        P("tok", "grp"),
        P("grp", "tok"),
        P("grp", "tok", None),
        P(None, "tok", None),
        P(),
        P(),
        P(),
    )
    out_specs = (P(("grp", "tok"), None), P(("grp", "tok"), None))
    return jax.shard_map(body, mesh=mesh, in_specs=in_specs, out_specs=out_specs, check_vma=False)
```

profile of v0, /device:TPU:1, one launch (start us, length us, event | category | flops | bytes accessed | tf_op | source)
XLA Modules:
  0.0 412.8 jit_solution(16430526760427926107)
XLA Ops:
  20.9 6.3 %collective-permute-start = (bf16[128,288]{0,1:T(8,128)(2,1)S(1)}, bf16[128,288]{0,1:T(8,128)(2,1)}, u32[]{:S(2)}, u32[]{:S(2)}) collective-permute-start(bf16[128,288]{0,1:T(8,128)(2,1)S(1)} %pad_maximum_fusion.1), channel_id=1, source_target_pairs={{0,4},{1,5},{2,6},{3,7},{4,8},{5,9},{6,10},{7,11},{8,12},{9,13},{1... | collective-permute-start | bytes 221192 | tf_op jit(solution)/shard_map/ppermute | solution.py:18
  27.2 3.2 multiply_reduce_fusion
  30.4 3.7 collective-permute-start.1
  36.4 4.5 %collective-permute-start.2 = (bf16[128,288]{0,1:T(8,128)(2,1)}, bf16[128,288]{0,1:T(8,128)(2,1)S(1)}, u32[]{:S(2)}, u32[]{:S(2)}) collective-permute-start(bf16[128,288]{0,1:T(8,128)(2,1)} %collective-permute-done.1), channel_id=1, source_target_pairs={{0,4},{1,5},{2,6},{3,7},{4,8},{5,9},{6,10},{7,11},{8,12},{9,13},{1... | collective-permute-start | bytes 221192 | tf_op jit(solution)/shard_map/ppermute | solution.py:18
  42.6 5.1 %collective-permute-start.3 = (bf16[128,288]{0,1:T(8,128)(2,1)S(1)}, bf16[128,288]{0,1:T(8,128)(2,1)S(1)}, u32[]{:S(2)}, u32[]{:S(2)}) collective-permute-start(bf16[128,288]{0,1:T(8,128)(2,1)S(1)} %collective-permute-done.2), channel_id=1, source_target_pairs={{0,4},{1,5},{2,6},{3,7},{4,8},{5,9},{6,10},{7,11},{8,12},{9,13},{1... | collective-permute-start | bytes 221192 | tf_op jit(solution)/shard_map/ppermute | solution.py:18
  47.7 2.9 collective-permute-done.3
  50.7 5.6 %collective-permute-start.4 = (bf16[128,288]{0,1:T(8,128)(2,1)S(1)}, bf16[128,288]{0,1:T(8,128)(2,1)S(1)}, u32[]{:S(2)}, u32[]{:S(2)}) collective-permute-start(bf16[128,288]{0,1:T(8,128)(2,1)S(1)} %collective-permute-done.3), channel_id=1, source_target_pairs={{0,4},{1,5},{2,6},{3,7},{4,8},{5,9},{6,10},{7,11},{8,12},{9,13},{1... | collective-permute-start | bytes 221192 | tf_op jit(solution)/shard_map/ppermute | solution.py:18
  62.0 6.0 %collective-permute-start.5 = (bf16[128,288]{0,1:T(8,128)(2,1)S(1)}, bf16[128,288]{0,1:T(8,128)(2,1)S(1)}, u32[]{:S(2)}, u32[]{:S(2)}) collective-permute-start(bf16[128,288]{0,1:T(8,128)(2,1)S(1)} %collective-permute-done.4), channel_id=1, source_target_pairs={{0,4},{1,5},{2,6},{3,7},{4,8},{5,9},{6,10},{7,11},{8,12},{9,13},{1... | collective-permute-start | bytes 221192 | tf_op jit(solution)/shard_map/ppermute | solution.py:18
  67.9 3.0 pad_maximum_fusion
  73.1 3.4 collective-permute-start.6
  87.5 26.8 %while.56 = (s32[]{:T(128)}, f32[2560]{0:T(1024)S(1)}, f32[2560]{0:T(1024)S(1)}, f32[2560,256]{1,0:T(8,128)S(1)}, bf16[1024,288]{1,0:T(8,128)(2,1)}, /*index=5*/...) while((s32[]{:T(128)}, f32[2560]{0:T(1024)S(1)}, ...), condition=%wide.region_5.6_spmd.clone, body=%wide.region_2.5_spmd.clone.sunk | while | flops 1439840768 | bytes 44730576 | solution.py:64
  88.0 5.6 %fusion.130 = (f32[2560]{0:T(1024)S(1)}, f32[512,2560]{1,0:T(8,128)}) fusion(pred[512]{0:T(512)(128)(4,1)S(1)} %fusion.129, bf16[2560,288]{1,0:T(8,128)(2,1)} %get-tuple-element.733, bf16[1024,288]{1,0:T(8,128)(2,1)} %get-tuple-element.732, s32[]{:T(128)S(6)} %select_n.152), kind=kOutput, calls=%fused_computation.53.clone.1 | convolution fusion | flops 758904320 | bytes 7612932 | tf_op jit(solution)/shard_map/while/body/eval_jaxpr/rw,kw->rk/dot_general | solution.py:50
  93.6 3.5 fusion.131
  97.7 2.9 convolution_add_fusion.9
  101.1 5.6 %fusion.130 = (f32[2560]{0:T(1024)S(1)}, f32[512,2560]{1,0:T(8,128)}) fusion(pred[512]{0:T(512)(128)(4,1)S(1)} %fusion.129, bf16[2560,288]{1,0:T(8,128)(2,1)} %get-tuple-element.733, bf16[1024,288]{1,0:T(8,128)(2,1)} %get-tuple-element.732, s32[]{:T(128)S(6)} %select_n.152), kind=kOutput, calls=%fused_computation.53.clone.1 | convolution fusion | flops 758904320 | bytes 7612932 | tf_op jit(solution)/shard_map/while/body/eval_jaxpr/rw,kw->rk/dot_general | solution.py:50
  106.8 3.5 fusion.131
  111.4 2.9 convolution_add_fusion.9
  114.3 14.3 %all-gather.9.cloned.1.call-done = bf16[4,4096,288]{1,2,0:T(8,128)(2,1)} async-done(((bf16[4,128,288]{1,2,0:T(8,128)(2,1)}), bf16[4,4096,288]{1,2,0:T(8,128)(2,1)}) %all-gather.9.cloned.1.call-update) | async-done | bytes 9437200 | tf_op jit(solution)/shard_map/all_gather | solution.py:134
  128.6 3.3 constant_dynamic-slice_fusion
  131.9 4.5 %copy.36 = bf16[1,4096,288]{2,1,0:T(8,128)(2,1)} copy(bf16[1,4096,288]{1,2,0:T(8,128)(2,1)} %constant_dynamic-slice_fusion) | data formatting | bytes 4718592 | tf_op jit(solution)/shard_map/jit(dynamic_index_in_dim)/dynamic_slice | solution.py:137
  136.4 61.9 %while.54 = (s32[]{:T(128)}, f32[2560]{0:T(1024)S(1)}, f32[2560]{0:T(1024)S(1)}, f32[2560,256]{1,0:T(8,128)S(1)}, bf16[4096,288]{1,0:T(8,128)(2,1)}, /*index=5*/...) while((s32[]{:T(128)}, f32[2560]{0:T(1024)S(1)}, ...), condition=%wide.region_9.10_spmd.clone, body=%wide.region_6.9_spmd.clone.sunk | while | flops 1439177728 | bytes 23759020 | solution.py:64
  137.0 3.3 fusion.119
  141.4 2.7 convolution_add_fusion.7
  144.7 3.3 fusion.119
  149.1 2.7 convolution_add_fusion.7
  152.5 3.3 fusion.119
  156.9 2.7 convolution_add_fusion.7
  160.2 3.3 fusion.119
  164.6 2.7 convolution_add_fusion.7
  167.9 3.4 fusion.119
  172.4 2.7 convolution_add_fusion.7
  175.7 3.3 fusion.119
  180.1 2.7 convolution_add_fusion.7
  183.5 3.3 fusion.119
  187.8 2.7 convolution_add_fusion.7
  191.2 3.3 fusion.119
  198.3 19.1 %while.55 = (s32[]{:T(128)}, f32[2560]{0:T(1024)S(1)}, f32[2560]{0:T(1024)S(1)}, f32[2560,256]{1,0:T(8,128)S(1)}, bf16[1024,288]{0,1:T(8,128)(2,1)}, /*index=5*/...) while((s32[]{:T(128)}, f32[2560]{0:T(1024)S(1)}, ...), condition=%wide.region_14.15_spmd.clone, body=%wide.region_11.14_spmd.clone.sunk | while | flops 1447041536 | bytes 23730872 | solution.py:64
  198.7 4.0 fusion.124
  204.6 3.3 convolution_add_fusion.8
  208.2 4.0 fusion.124
  214.1 3.3 convolution_add_fusion.8
  221.9 3.9 fusion.59
  228.6 32.8 %all-gather.11.cloned.1.call-done = bf16[512,2560]{1,0:T(8,128)(2,1)} async-done(((bf16[128,2560]{1,0:T(8,128)(2,1)}), bf16[512,2560]{1,0:T(8,128)(2,1)}) %all-gather.11.cloned.1.call-update) | async-done | bytes 2621456 | tf_op jit(solution)/shard_map/all_gather | solution.py:180
  261.4 6.7 %fusion.81 = f32[512,800]{0,1:T(8,128)} fusion(bf16[512,2560]{1,0:T(8,128)(2,1)} %all-gather.11.cloned.1.call-done, bf16[2560,800]{1,0:T(8,128)(2,1)} %all-gather.13.cloned.1.call-done), kind=kOutput, calls=%fused_computation.136 | convolution fusion | flops 2097152000 | bytes 8355840 | tf_op jit(solution)/shard_map/dot_general | solution.py:181
  268.1 42.8 %all-gather.15.cloned.1.call-done = bf16[2560,800]{1,0:T(8,128)(2,1)} async-done(((bf16[80,800]{1,0:T(8,128)(2,1)}), bf16[2560,800]{1,0:T(8,128)(2,1)}) %all-gather.15.cloned.1.call-update) | async-done | bytes 4096016 | tf_op jit(solution)/shard_map/all_gather | solution.py:188
  310.9 48.1 %all-gather.17.cloned.1.call-done = bf16[800,2560]{0,1:T(8,128)(2,1)} async-done(((bf16[800,80]{0,1:T(8,128)(2,1)}), bf16[800,2560]{0,1:T(8,128)(2,1)}) %all-gather.17.cloned.1.call-update) | async-done | bytes 4096016 | tf_op jit(solution)/shard_map/all_gather | solution.py:194
  358.9 11.8 %convolution_convert_fusion = bf16[512,2560]{1,0:T(8,128)(2,1)} fusion(bf16[800,2560]{0,1:T(8,128)(2,1)} %all-gather.17.cloned.1.call-done, f32[512,800]{0,1:T(8,128)} %fusion.81, bf16[512,2560]{1,0:T(8,128)(2,1)} %all-gather.11.cloned.1.call-done, bf16[2560,800]{1,0:T(8,128)(2,1)} %all-gather.15.cloned.1.call-done), kind=kOutput, calls=%fused_computation.77 | convolution fusion | flops 4198072320 | bytes 15073280 | tf_op jit(solution)/shard_map/dot_general | solution.py:192
  370.7 32.9 %reduce-scatter.2.cloned.1.call-done = bf16[128,2560]{1,0:T(8,128)(2,1)} async-done(((bf16[512,2560]{1,0:T(8,128)(2,1)}), bf16[128,2560]{1,0:T(8,128)(2,1)}) %reduce-scatter.2.cloned.1.call-update) | async-done | bytes 655376 | tf_op jit(solution)/shard_map/reduce_scatter | solution.py:197
  (160 shorter events, 65.5 us)
Async XLA Ops:
  7.2 26.9 %copy-start = (bf16[768,1920]{1,0:T(8,128)(2,1)S(1)}, bf16[768,1920]{1,0:T(8,128)(2,1)}, u32[]{:S(2)}) copy-start(bf16[768,1920]{1,0:T(8,128)(2,1)} %param.29) | copy-start | bytes 8847364
  7.2 78.2 %all-gather.7.cloned.1.call-start = ((), (), s32[]{:S(2)}) async-start(), calls=%async_computation.1 | async-start | bytes 6488064 | tf_op jit(solution)/shard_map/all_gather | solution.py:135
  7.9 120.7 %all-gather.9.cloned.1.call-start = ((), (), s32[]{:S(2)}) async-start(), calls=%async_computation.2 | async-start | bytes 9732096 | tf_op jit(solution)/shard_map/all_gather | solution.py:134
  8.7 219.9 %all-gather.13.cloned.1.call-start = ((), (), s32[]{:S(2)}) async-start(), calls=%async_computation.4 | async-start | bytes 4730880 | tf_op jit(solution)/shard_map/all_gather | solution.py:183
  20.8 9.6 %copy-start.8 = (bf16[768]{0:T(1024)(128)(2,1)S(1)}, bf16[768]{0:T(1024)(128)(2,1)}, u32[]{:S(2)}) copy-start(bf16[768]{0:T(1024)(128)(2,1)} %param.28) | copy-start | bytes 4612
  20.8 13.3 %copy-start.6 = (bf16[128,288]{0,1:T(8,128)(2,1)}, bf16[128,288]{0,1:T(8,128)(2,1)S(1)}, u32[]{:S(2)}) copy-start(bf16[128,288]{0,1:T(8,128)(2,1)S(1)} %pad_maximum_fusion.1) | copy-start | bytes 221188
  20.9 9.6 %collective-permute-start = (bf16[128,288]{0,1:T(8,128)(2,1)S(1)}, bf16[128,288]{0,1:T(8,128)(2,1)}, u32[]{:S(2)}, u32[]{:S(2)}) collective-permute-start(bf16[128,288]{0,1:T(8,128)(2,1)S(1)} %pad_maximum_fusion.1), channel_id=1, source_target_pairs={{0,4},{1,5},{2,6},{3,7},{4,8},{5,9},{6,10},{7,11},{8,12},{9,13},{1... | collective-permute-start | bytes 221192 | tf_op jit(solution)/shard_map/ppermute | solution.py:18
  27.1 234.2 %all-gather.11.cloned.1.call-start = ((), (), s32[]{:S(2)}) async-start(), calls=%async_computation.3 | async-start | bytes 3276800 | tf_op jit(solution)/shard_map/all_gather | solution.py:180
  30.4 5.9 %collective-permute-start.1 = (bf16[128,288]{0,1:T(8,128)(2,1)}, bf16[128,288]{0,1:T(8,128)(2,1)}, u32[]{:S(2)}, u32[]{:S(2)}) collective-permute-start(bf16[128,288]{0,1:T(8,128)(2,1)} %collective-permute-done), channel_id=1, source_target_pairs={{0,4},{1,5},{2,6},{3,7},{4,8},{5,9},{6,10},{7,11},{8,12},{9,13},{1... | collective-permute-start | bytes 221192 | tf_op jit(solution)/shard_map/ppermute | solution.py:18
  36.4 6.2 %collective-permute-start.2 = (bf16[128,288]{0,1:T(8,128)(2,1)}, bf16[128,288]{0,1:T(8,128)(2,1)S(1)}, u32[]{:S(2)}, u32[]{:S(2)}) collective-permute-start(bf16[128,288]{0,1:T(8,128)(2,1)} %collective-permute-done.1), channel_id=1, source_target_pairs={{0,4},{1,5},{2,6},{3,7},{4,8},{5,9},{6,10},{7,11},{8,12},{9,13},{1... | collective-permute-start | bytes 221192 | tf_op jit(solution)/shard_map/ppermute | solution.py:18
  42.6 8.1 %collective-permute-start.3 = (bf16[128,288]{0,1:T(8,128)(2,1)S(1)}, bf16[128,288]{0,1:T(8,128)(2,1)S(1)}, u32[]{:S(2)}, u32[]{:S(2)}) collective-permute-start(bf16[128,288]{0,1:T(8,128)(2,1)S(1)} %collective-permute-done.2), channel_id=1, source_target_pairs={{0,4},{1,5},{2,6},{3,7},{4,8},{5,9},{6,10},{7,11},{8,12},{9,13},{1... | collective-permute-start | bytes 221192 | tf_op jit(solution)/shard_map/ppermute | solution.py:18
  50.7 11.3 %collective-permute-start.4 = (bf16[128,288]{0,1:T(8,128)(2,1)S(1)}, bf16[128,288]{0,1:T(8,128)(2,1)S(1)}, u32[]{:S(2)}, u32[]{:S(2)}) collective-permute-start(bf16[128,288]{0,1:T(8,128)(2,1)S(1)} %collective-permute-done.3), channel_id=1, source_target_pairs={{0,4},{1,5},{2,6},{3,7},{4,8},{5,9},{6,10},{7,11},{8,12},{9,13},{1... | collective-permute-start | bytes 221192 | tf_op jit(solution)/shard_map/ppermute | solution.py:18
  62.0 11.2 %copy-start.7 = (bf16[2560]{0:T(1024)(128)(2,1)S(1)}, bf16[2560]{0:T(1024)(128)(2,1)}, u32[]{:S(2)}) copy-start(bf16[2560]{0:T(1024)(128)(2,1)} %param.35) | copy-start | bytes 15364
  62.0 11.2 %collective-permute-start.5 = (bf16[128,288]{0,1:T(8,128)(2,1)S(1)}, bf16[128,288]{0,1:T(8,128)(2,1)S(1)}, u32[]{:S(2)}, u32[]{:S(2)}) collective-permute-start(bf16[128,288]{0,1:T(8,128)(2,1)S(1)} %collective-permute-done.4), channel_id=1, source_target_pairs={{0,4},{1,5},{2,6},{3,7},{4,8},{5,9},{6,10},{7,11},{8,12},{9,13},{1... | collective-permute-start | bytes 221192 | tf_op jit(solution)/shard_map/ppermute | solution.py:18
  73.1 5.2 %collective-permute-start.6 = (bf16[128,288]{0,1:T(8,128)(2,1)S(1)}, bf16[128,288]{0,1:T(8,128)(2,1)S(1)}, u32[]{:S(2)}, u32[]{:S(2)}) collective-permute-start(bf16[128,288]{0,1:T(8,128)(2,1)S(1)} %collective-permute-done.5), channel_id=1, source_target_pairs={{0,4},{1,5},{2,6},{3,7},{4,8},{5,9},{6,10},{7,11},{8,12},{9,13},{1... | collective-permute-start | bytes 221192 | tf_op jit(solution)/shard_map/ppermute | solution.py:18
  93.6 4.0 copy-start.2
  106.8 4.7 %copy-start.2 = (f32[512,2560]{1,0:T(8,128)S(1)}, f32[512,2560]{1,0:T(8,128)}, u32[]{:S(2)}) copy-start(f32[512,2560]{1,0:T(8,128)} %get-tuple-element.703) | copy-start | bytes 15728644 | tf_op jit(solution)/shard_map/while
  218.9 2.3 copy-start.5
  218.9 2.9 copy-start.4
  225.8 42.3 %copy-start.3 = (bf16[128,2560]{1,0:T(8,128)(2,1)}, bf16[128,2560]{1,0:T(8,128)(2,1)S(1)}, u32[]{:S(2)}) copy-start(bf16[128,2560]{1,0:T(8,128)(2,1)S(1)} %fusion.59) | copy-start | bytes 1966084
  227.1 83.7 %all-gather.15.cloned.1.call-start = ((), (), s32[]{:S(2)}) async-start(), calls=%async_computation.5 | async-start | bytes 4730880 | tf_op jit(solution)/shard_map/all_gather | solution.py:188
  227.7 131.2 %all-gather.17.cloned.1.call-start = ((), (), s32[]{:S(2)}) async-start(), calls=%async_computation.6 | async-start | bytes 4730880 | tf_op jit(solution)/shard_map/all_gather | solution.py:194
  228.3 175.4 %reduce-scatter.2.cloned.1.call-start = ((), (), s32[]{:S(2)}) async-start(), calls=%async_computation.7 | async-start | bytes 3276800 | tf_op jit(solution)/shard_map/reduce_scatter | solution.py:197
  358.9 47.0 %copy-start.1 = (bf16[768,1920]{1,0:T(8,128)(2,1)S(1)}, bf16[768,1920]{1,0:T(8,128)(2,1)}, u32[]{:S(2)}) copy-start(bf16[768,1920]{1,0:T(8,128)(2,1)} %param.29) | copy-start | bytes 8847364
Sparse Core Ops, SparseCore 0:
  10.3 55.2 all-gather.6
  67.7 60.8 all-gather.8
  130.9 46.1 all-gather.12
  227.2 34.1 all-gather.10
  263.6 47.2 all-gather.14
  313.0 45.8 all-gather.16
  370.9 32.7 reduce-scatter.1
where the time goes:
time: 415 us; the launch traced here: 413 us
  waiting for transfers between devices  179 us (43%)
  matrix products  109 us (26%)
  other arithmetic  37.2 us (9%)
  starting transfers between devices  35.1 us (8%)
  local copies, waits for them, and re-layouts  33.7 us (8%)
  between operations  17.6 us (4%)
    all_gather x1, waiting for transfers between devices, body(): lax.all_gather(down_weight, 'tok', axis=1, tiled=True)  48.1 us
    dot_general x12, matrix products, fold_block(): jnp.einsum('rw,kw->rk', queries, key_piece, preferred_element_type=jnp.fl...  45.9 us
    all_gather x1, waiting for transfers between devices, body(): lax.all_gather(up_weight, 'tok', axis=0, tiled=True)  42.8 us
    ppermute x7, starting transfers between devices, passed_along(): return lax.ppermute(block, axis, route)  34.6 us
    dot_general x12, matrix products, fold_block(): jnp.dot(weights.astype(jnp.bfloat16), key_piece[:, :KVR], preferred_eleme...  33.7 us
    reduce_scatter x1, waiting for transfers between devices, body(): lax.psum_scatter(partial_out.astype(jnp.bfloat16), 'grp', scatter_dimensi...  32.9 us
    all_gather x1, waiting for transfers between devices, body(): rows_all = lax.all_gather(post_norm, 'grp', axis=0, tiled=True)  32.8 us
    reduce_sum x12, other arithmetic, fold_block(): running_sum = running_sum * factor + jnp.sum(weights, axis=1)  19 us
  transfers between devices with their start and end apart: 14, of which 8 were waited for; matrix products, arithmetic and copies ran while one was open for 40% of the time, Pallas kernels for 0%

commit v1 on v0

--- a/solution.py
+++ b/solution.py
@@ -1,3 +1,4 @@
+import functools
 import jax
 import jax.numpy as jnp
 from jax import lax
@@ -10,6 +11,28 @@
 VDIM = 64
 SPAN = 1024
 EPSILON = 1e-06
+
+
+def map_point(row_data, peer_axis, along_dim):
+    count_all = jax.lax.axis_size(peer_axis)
+    runs = [(j0, (j0 + 1) % count_all) for j0 in range(count_all)]
+    panels = [(j0, (j0 - 1) % count_all) for j0 in range(count_all)]
+    t1, small = ([row_data], [row_data])
+    for _ in range(count_all // 2):
+        t1.append(jax.lax.ppermute(t1[-1], peer_axis, runs))
+    for _ in range((count_all - 1) // 2):
+        base_arr = jax.lax.ppermute(small[-1], peer_axis, panels)
+        small.append(base_arr)
+    r2 = jnp.concatenate([*t1[::-1], *small[1:]], axis=along_dim)
+    latest = jnp.roll(
+        r2,
+        shift=(jax.lax.axis_index(peer_axis) - count_all // 2) * row_data.shape[along_dim],
+        axis=along_dim,
+    )
+    return latest
+
+
+proceed_links = functools.partial(map_point, peer_axis="grp", along_dim=0)
 
 
 def passed_along(block, axis, distance):
@@ -177,7 +200,7 @@
         (tokens.astype(jnp.float32) + attended).astype(jnp.bfloat16)
     )
     post_norm = norm_rows(residual.astype(jnp.float32), post_gain).astype(jnp.bfloat16)
-    rows_all = lax.all_gather(post_norm, "grp", axis=0, tiled=True)
+    rows_all = proceed_links(post_norm)
     gate_values = jnp.dot(
         rows_all,
         lax.all_gather(gate_weight, "tok", axis=0, tiled=True),

time: 415 us -> 332 us (0.80)
  waiting for transfers between devices: 179 us -> 83.7 us
  local copies, waits for them, and re-layouts: 33.7 us -> 38.6 us
  starting transfers between devices: 35.1 us -> 39.4 us
    all_gather x1, waiting for transfers between devices: 48.1 us -> 0.01 us  [body(): lax.all_gather(down_weight, 'tok', axis=1, tiled=True)]
    all_gather x1, waiting for transfers between devices: 42.8 us -> 0.01 us  [body(): lax.all_gather(up_weight, 'tok', axis=0, tiled=True)]
    all_gather x1 -> x0, waiting for transfers between devices: 32.8 us -> none  [body(): rows_all = lax.all_gather(post_norm, 'grp', axis=0, tiled=True)]
    ppermute x0 -> x3, waiting for transfers between devices: none -> 29.7 us  [the longest x2 29.7 us: map_point(): t1.append(jax.lax.ppermute(t1[-1], peer_axis, runs))]
    unnamed x25 -> x32, local copies, waits for them, and re-layouts: 9.84 us -> 14.2 us
  transfers between devices with their start and end apart: 14 -> 16, of which waited for: 8 -> 7; matrix products, arithmetic and copies ran while one was open for 40% -> 52% of each run, Pallas kernels for 0% -> 0%
where the time goes in v1:
time: 332 us; the launch traced here: 330 us
  matrix products  109 us (33%)
  waiting for transfers between devices  83.7 us (25%)
  other arithmetic  39.8 us (12%)
  starting transfers between devices  39.4 us (12%)
  local copies, waits for them, and re-layouts  38.6 us (12%)
  between operations  17.8 us (5%)
    dot_general x12, matrix products, fold_block(): jnp.einsum('rw,kw->rk', queries, key_piece, preferred_element_type=jnp.fl...  46.1 us
    ppermute x7, starting transfers between devices, passed_along(): return lax.ppermute(block, axis, route)  35.2 us
    dot_general x12, matrix products, fold_block(): jnp.dot(weights.astype(jnp.bfloat16), key_piece[:, :KVR], preferred_eleme...  33.7 us
    reduce_scatter x1, waiting for transfers between devices, body(): lax.psum_scatter(partial_out.astype(jnp.bfloat16), 'grp', scatter_dimensi...  32.6 us
    ppermute x2, waiting for transfers between devices, map_point(): t1.append(jax.lax.ppermute(t1[-1], peer_axis, runs))  29.7 us
    reduce_sum x12, other arithmetic, fold_block(): running_sum = running_sum * factor + jnp.sum(weights, axis=1)  19.6 us
    unnamed x32, local copies, waits for them, and re-layouts  14.2 us
    all_gather x1, waiting for transfers between devices, body(): lax.all_gather(cache_latents, 'tok', axis=1, tiled=True)  12.7 us
  transfers between devices with their start and end apart: 16, of which 7 were waited for; matrix products, arithmetic and copies ran while one was open for 52% of the time, Pallas kernels for 0%

profile of v1, /device:TPU:1, one launch (start us, length us, event | category | flops | bytes accessed | tf_op | source)
XLA Modules:
  0.0 329.7 jit_solution(16423033308081365565)
XLA Ops:
  22.5 6.3 %collective-permute-start = (bf16[128,288]{0,1:T(8,128)(2,1)S(1)}, bf16[128,288]{0,1:T(8,128)(2,1)}, u32[]{:S(2)}, u32[]{:S(2)}) collective-permute-start(bf16[128,288]{0,1:T(8,128)(2,1)S(1)} %pad_maximum_fusion.1), channel_id=1, source_target_pairs={{0,4},{1,5},{2,6},{3,7},{4,8},{5,9},{6,10},{7,11},{8,12},{9,13},{1... | collective-permute-start | bytes 221192 | tf_op jit(solution)/shard_map/ppermute | solution.py:41
  28.8 3.1 multiply_reduce_fusion
  32.0 4.5 %collective-permute-start.1 = (bf16[128,288]{0,1:T(8,128)(2,1)}, bf16[128,288]{0,1:T(8,128)(2,1)}, u32[]{:S(2)}, u32[]{:S(2)}) collective-permute-start(bf16[128,288]{0,1:T(8,128)(2,1)} %collective-permute-done), channel_id=1, source_target_pairs={{0,4},{1,5},{2,6},{3,7},{4,8},{5,9},{6,10},{7,11},{8,12},{9,13},{1... | collective-permute-start | bytes 221192 | tf_op jit(solution)/shard_map/ppermute | solution.py:41
  38.8 4.0 %collective-permute-start.2 = (bf16[128,288]{0,1:T(8,128)(2,1)}, bf16[128,288]{0,1:T(8,128)(2,1)S(1)}, u32[]{:S(2)}, u32[]{:S(2)}) collective-permute-start(bf16[128,288]{0,1:T(8,128)(2,1)} %collective-permute-done.1), channel_id=1, source_target_pairs={{0,4},{1,5},{2,6},{3,7},{4,8},{5,9},{6,10},{7,11},{8,12},{9,13},{1... | collective-permute-start | bytes 221192 | tf_op jit(solution)/shard_map/ppermute | solution.py:41
  44.5 5.1 %collective-permute-start.3 = (bf16[128,288]{0,1:T(8,128)(2,1)S(1)}, bf16[128,288]{0,1:T(8,128)(2,1)S(1)}, u32[]{:S(2)}, u32[]{:S(2)}) collective-permute-start(bf16[128,288]{0,1:T(8,128)(2,1)S(1)} %collective-permute-done.2), channel_id=1, source_target_pairs={{0,4},{1,5},{2,6},{3,7},{4,8},{5,9},{6,10},{7,11},{8,12},{9,13},{1... | collective-permute-start | bytes 221192 | tf_op jit(solution)/shard_map/ppermute | solution.py:41
  51.8 5.7 %collective-permute-start.4 = (bf16[128,288]{0,1:T(8,128)(2,1)S(1)}, bf16[128,288]{0,1:T(8,128)(2,1)S(1)}, u32[]{:S(2)}, u32[]{:S(2)}) collective-permute-start(bf16[128,288]{0,1:T(8,128)(2,1)S(1)} %collective-permute-done.3), channel_id=1, source_target_pairs={{0,4},{1,5},{2,6},{3,7},{4,8},{5,9},{6,10},{7,11},{8,12},{9,13},{1... | collective-permute-start | bytes 221192 | tf_op jit(solution)/shard_map/ppermute | solution.py:41
  63.2 5.9 %collective-permute-start.5 = (bf16[128,288]{0,1:T(8,128)(2,1)S(1)}, bf16[128,288]{0,1:T(8,128)(2,1)S(1)}, u32[]{:S(2)}, u32[]{:S(2)}) collective-permute-start(bf16[128,288]{0,1:T(8,128)(2,1)S(1)} %collective-permute-done.4), channel_id=1, source_target_pairs={{0,4},{1,5},{2,6},{3,7},{4,8},{5,9},{6,10},{7,11},{8,12},{9,13},{1... | collective-permute-start | bytes 221192 | tf_op jit(solution)/shard_map/ppermute | solution.py:41
  69.1 3.0 pad_maximum_fusion
  74.2 3.8 %collective-permute-start.6 = (bf16[128,288]{0,1:T(8,128)(2,1)S(1)}, bf16[128,288]{0,1:T(8,128)(2,1)S(1)}, u32[]{:S(2)}, u32[]{:S(2)}) collective-permute-start(bf16[128,288]{0,1:T(8,128)(2,1)S(1)} %collective-permute-done.5), channel_id=1, source_target_pairs={{0,4},{1,5},{2,6},{3,7},{4,8},{5,9},{6,10},{7,11},{8,12},{9,13},{1... | collective-permute-start | bytes 221192 | tf_op jit(solution)/shard_map/ppermute | solution.py:41
  78.0 2.8 collective-permute-done.6
  89.8 27.4 %while.56 = (s32[]{:T(128)}, f32[2560]{0:T(1024)S(1)}, f32[2560]{0:T(1024)S(1)}, f32[2560,256]{1,0:T(8,128)S(1)}, bf16[1024,288]{1,0:T(8,128)(2,1)}, /*index=5*/...) while((s32[]{:T(128)}, f32[2560]{0:T(1024)S(1)}, ...), condition=%wide.region_5.6_spmd.clone, body=%wide.region_2.5_spmd.clone.sunk | while | flops 1439840768 | bytes 44730576 | solution.py:87
  90.5 5.7 %fusion.139 = (f32[2560]{0:T(1024)S(1)}, f32[512,2560]{1,0:T(8,128)}) fusion(pred[512]{0:T(512)(128)(4,1)S(1)} %fusion.138, bf16[2560,288]{1,0:T(8,128)(2,1)} %get-tuple-element.733, bf16[1024,288]{1,0:T(8,128)(2,1)} %get-tuple-element.732, s32[]{:T(128)S(6)} %select_n.166), kind=kOutput, calls=%fused_computation.53.clone.1 | convolution fusion | flops 758904320 | bytes 7612932 | tf_op jit(solution)/shard_map/while/body/eval_jaxpr/rw,kw->rk/dot_general | solution.py:73
  96.2 3.5 %fusion.140 = f32[2560]{0:T(1024)S(1)} fusion(f32[512,2560]{1,0:T(8,128)} %get-tuple-element.703, f32[2560]{0:T(1024)S(1)} %select_maximum_fusion.2, pred[512]{0:T(512)(128)(4,1)S(1)} %fusion.138), kind=kLoop, calls=%fused_computation.58.clone.1 | loop fusion | flops 3929600 | bytes 5263872 | tf_op jit(solution)/shard_map/while/body/eval_jaxpr/reduce_sum | solution.py:81
  100.3 2.9 convolution_add_fusion.9
  103.9 5.7 %fusion.139 = (f32[2560]{0:T(1024)S(1)}, f32[512,2560]{1,0:T(8,128)}) fusion(pred[512]{0:T(512)(128)(4,1)S(1)} %fusion.138, bf16[2560,288]{1,0:T(8,128)(2,1)} %get-tuple-element.733, bf16[1024,288]{1,0:T(8,128)(2,1)} %get-tuple-element.732, s32[]{:T(128)S(6)} %select_n.166), kind=kOutput, calls=%fused_computation.53.clone.1 | convolution fusion | flops 758904320 | bytes 7612932 | tf_op jit(solution)/shard_map/while/body/eval_jaxpr/rw,kw->rk/dot_general | solution.py:73
  109.6 4.2 %fusion.140 = f32[2560]{0:T(1024)S(1)} fusion(f32[512,2560]{1,0:T(8,128)} %get-tuple-element.703, f32[2560]{0:T(1024)S(1)} %select_maximum_fusion.2, pred[512]{0:T(512)(128)(4,1)S(1)} %fusion.138), kind=kLoop, calls=%fused_computation.58.clone.1 | loop fusion | flops 3929600 | bytes 5263872 | tf_op jit(solution)/shard_map/while/body/eval_jaxpr/reduce_sum | solution.py:81
  114.4 2.9 convolution_add_fusion.9
  117.3 12.7 %all-gather.8.cloned.1.call-done = bf16[4,4096,288]{1,2,0:T(8,128)(2,1)} async-done(((bf16[4,128,288]{1,2,0:T(8,128)(2,1)}), bf16[4,4096,288]{1,2,0:T(8,128)(2,1)}) %all-gather.8.cloned.1.call-update) | async-done | bytes 9437200 | tf_op jit(solution)/shard_map/all_gather | solution.py:157
  130.0 3.3 %constant_dynamic-slice_fusion = bf16[1,4096,288]{1,2,0:T(8,128)(2,1)} fusion(bf16[4,4096,288]{1,2,0:T(8,128)(2,1)} %all-gather.8.cloned.1.call-done, s32[]{:T(128)S(6)} %select_n.104), kind=kLoop, calls=%fused_computation.142 | loop fusion | bytes 4718596 | tf_op jit(solution)/shard_map/jit(dynamic_index_in_dim)/dynamic_slice | solution.py:160
  133.3 4.5 %copy.36 = bf16[1,4096,288]{2,1,0:T(8,128)(2,1)} copy(bf16[1,4096,288]{1,2,0:T(8,128)(2,1)} %constant_dynamic-slice_fusion) | data formatting | bytes 4718592 | tf_op jit(solution)/shard_map/jit(dynamic_index_in_dim)/dynamic_slice | solution.py:160
  137.8 62.4 %while.54 = (s32[]{:T(128)}, f32[2560]{0:T(1024)S(1)}, f32[2560]{0:T(1024)S(1)}, f32[2560,256]{1,0:T(8,128)S(1)}, bf16[4096,288]{1,0:T(8,128)(2,1)}, /*index=5*/...) while((s32[]{:T(128)}, f32[2560]{0:T(1024)S(1)}, ...), condition=%wide.region_9.10_spmd.clone, body=%wide.region_6.9_spmd.clone.sunk | while | flops 1439177728 | bytes 23759020 | solution.py:87
  138.5 3.3 %fusion.128 = (f32[2560]{0:T(1024)S(1)}, f32[512,2560]{1,0:T(8,128)S(1)}) fusion(pred[512]{0:T(512)(128)(4,1)S(1)} %fusion.127, bf16[2560,288]{1,0:T(8,128)(2,1)} %get-tuple-element.766, bf16[4096,288]{1,0:T(8,128)(2,1)} %get-tuple-element.765, s32[]{:T(128)S(6)} %select_n.158), kind=kOutput, calls=%fused_computation.6.clone.1 | convolution fusion | flops 758904320 | bytes 7612932 | tf_op jit(solution)/shard_map/while/body/eval_jaxpr/rw,kw->rk/dot_general | solution.py:73
  142.9 2.7 convolution_add_fusion.7
  146.2 3.3 %fusion.128 = (f32[2560]{0:T(1024)S(1)}, f32[512,2560]{1,0:T(8,128)S(1)}) fusion(pred[512]{0:T(512)(128)(4,1)S(1)} %fusion.127, bf16[2560,288]{1,0:T(8,128)(2,1)} %get-tuple-element.766, bf16[4096,288]{1,0:T(8,128)(2,1)} %get-tuple-element.765, s32[]{:T(128)S(6)} %select_n.158), kind=kOutput, calls=%fused_computation.6.clone.1 | convolution fusion | flops 758904320 | bytes 7612932 | tf_op jit(solution)/shard_map/while/body/eval_jaxpr/rw,kw->rk/dot_general | solution.py:73
  154.0 3.3 %fusion.128 = (f32[2560]{0:T(1024)S(1)}, f32[512,2560]{1,0:T(8,128)S(1)}) fusion(pred[512]{0:T(512)(128)(4,1)S(1)} %fusion.127, bf16[2560,288]{1,0:T(8,128)(2,1)} %get-tuple-element.766, bf16[4096,288]{1,0:T(8,128)(2,1)} %get-tuple-element.765, s32[]{:T(128)S(6)} %select_n.158), kind=kOutput, calls=%fused_computation.6.clone.1 | convolution fusion | flops 758904320 | bytes 7612932 | tf_op jit(solution)/shard_map/while/body/eval_jaxpr/rw,kw->rk/dot_general | solution.py:73
  158.4 2.7 convolution_add_fusion.7
  161.8 3.3 %fusion.128 = (f32[2560]{0:T(1024)S(1)}, f32[512,2560]{1,0:T(8,128)S(1)}) fusion(pred[512]{0:T(512)(128)(4,1)S(1)} %fusion.127, bf16[2560,288]{1,0:T(8,128)(2,1)} %get-tuple-element.766, bf16[4096,288]{1,0:T(8,128)(2,1)} %get-tuple-element.765, s32[]{:T(128)S(6)} %select_n.158), kind=kOutput, calls=%fused_computation.6.clone.1 | convolution fusion | flops 758904320 | bytes 7612932 | tf_op jit(solution)/shard_map/while/body/eval_jaxpr/rw,kw->rk/dot_general | solution.py:73
  166.2 2.7 convolution_add_fusion.7
  169.6 3.4 %fusion.128 = (f32[2560]{0:T(1024)S(1)}, f32[512,2560]{1,0:T(8,128)S(1)}) fusion(pred[512]{0:T(512)(128)(4,1)S(1)} %fusion.127, bf16[2560,288]{1,0:T(8,128)(2,1)} %get-tuple-element.766, bf16[4096,288]{1,0:T(8,128)(2,1)} %get-tuple-element.765, s32[]{:T(128)S(6)} %select_n.158), kind=kOutput, calls=%fused_computation.6.clone.1 | convolution fusion | flops 758904320 | bytes 7612932 | tf_op jit(solution)/shard_map/while/body/eval_jaxpr/rw,kw->rk/dot_general | solution.py:73
  174.1 2.7 convolution_add_fusion.7
  177.5 3.3 %fusion.128 = (f32[2560]{0:T(1024)S(1)}, f32[512,2560]{1,0:T(8,128)S(1)}) fusion(pred[512]{0:T(512)(128)(4,1)S(1)} %fusion.127, bf16[2560,288]{1,0:T(8,128)(2,1)} %get-tuple-element.766, bf16[4096,288]{1,0:T(8,128)(2,1)} %get-tuple-element.765, s32[]{:T(128)S(6)} %select_n.158), kind=kOutput, calls=%fused_computation.6.clone.1 | convolution fusion | flops 758904320 | bytes 7612932 | tf_op jit(solution)/shard_map/while/body/eval_jaxpr/rw,kw->rk/dot_general | solution.py:73
  181.9 2.7 convolution_add_fusion.7
  185.3 3.3 %fusion.128 = (f32[2560]{0:T(1024)S(1)}, f32[512,2560]{1,0:T(8,128)S(1)}) fusion(pred[512]{0:T(512)(128)(4,1)S(1)} %fusion.127, bf16[2560,288]{1,0:T(8,128)(2,1)} %get-tuple-element.766, bf16[4096,288]{1,0:T(8,128)(2,1)} %get-tuple-element.765, s32[]{:T(128)S(6)} %select_n.158), kind=kOutput, calls=%fused_computation.6.clone.1 | convolution fusion | flops 758904320 | bytes 7612932 | tf_op jit(solution)/shard_map/while/body/eval_jaxpr/rw,kw->rk/dot_general | solution.py:73
  189.7 2.7 convolution_add_fusion.7
  193.1 3.3 %fusion.128 = (f32[2560]{0:T(1024)S(1)}, f32[512,2560]{1,0:T(8,128)S(1)}) fusion(pred[512]{0:T(512)(128)(4,1)S(1)} %fusion.127, bf16[2560,288]{1,0:T(8,128)(2,1)} %get-tuple-element.766, bf16[4096,288]{1,0:T(8,128)(2,1)} %get-tuple-element.765, s32[]{:T(128)S(6)} %select_n.158), kind=kOutput, calls=%fused_computation.6.clone.1 | convolution fusion | flops 758904320 | bytes 7612932 | tf_op jit(solution)/shard_map/while/body/eval_jaxpr/rw,kw->rk/dot_general | solution.py:73
  197.4 2.7 convolution_add_fusion.7
  200.1 19.1 %while.55 = (s32[]{:T(128)}, f32[2560]{0:T(1024)S(1)}, f32[2560]{0:T(1024)S(1)}, f32[2560,256]{1,0:T(8,128)S(1)}, bf16[1024,288]{0,1:T(8,128)(2,1)}, /*index=5*/...) while((s32[]{:T(128)}, f32[2560]{0:T(1024)S(1)}, ...), condition=%wide.region_14.15_spmd.clone, body=%wide.region_11.14_spmd.clone.sunk | while | flops 1447041536 | bytes 23730872 | solution.py:87
  200.6 4.0 %fusion.133 = (f32[2560]{0:T(1024)S(1)}, f32[512,2560]{1,0:T(8,128)S(1)}) fusion(s32[2560]{0:T(1024)S(1)} %lt.216, s32[512]{0:T(512)S(1)} %iota_add_fusion.5, pred[512]{0:T(512)(128)(4,1)S(1)} %broadcast_compare_fusion.2, bf16[2560,288]{1,0:T(8,128)(2,1)} %get-tuple-element.801, bf16[1024,288]{0,1:T(8,128)(2,1)} %get-tuple-element.800, ...), kind=kOutput, calls=%fused_computation.29.clone.1 | convolution fusion | flops 761525760 | bytes 7526916 | tf_op jit(solution)/shard_map/while/body/eval_jaxpr/rw,kw->rk/dot_general | solution.py:73
  206.5 3.3 convolution_add_fusion.8
  210.1 4.0 %fusion.133 = (f32[2560]{0:T(1024)S(1)}, f32[512,2560]{1,0:T(8,128)S(1)}) fusion(s32[2560]{0:T(1024)S(1)} %lt.216, s32[512]{0:T(512)S(1)} %iota_add_fusion.5, pred[512]{0:T(512)(128)(4,1)S(1)} %broadcast_compare_fusion.2, bf16[2560,288]{1,0:T(8,128)(2,1)} %get-tuple-element.801, bf16[1024,288]{0,1:T(8,128)(2,1)} %get-tuple-element.800, ...), kind=kOutput, calls=%fused_computation.29.clone.1 | convolution fusion | flops 761525760 | bytes 7526916 | tf_op jit(solution)/shard_map/while/body/eval_jaxpr/rw,kw->rk/dot_general | solution.py:73
  216.0 3.3 convolution_add_fusion.8
  223.8 3.9 %fusion.59 = bf16[128,2560]{1,0:T(8,128)(2,1)S(1)} fusion(bf16[128,1280]{0,1:T(8,128)(2,1)S(1)} %bitcast.101, bf16[1280,2560]{1,0:T(8,128)(2,1)} %param.34, bf16[128,2560]{1,0:T(8,128)(2,1)S(1)} %copy-done.4), kind=kOutput, calls=%fused_computation.79 | convolution fusion | flops 839843840 | bytes 8192000 | tf_op jit(solution)/shard_map/dot_general | solution.py:198
  229.4 16.0 %collective-permute-done.7 = bf16[128,2560]{1,0:T(8,128)(2,1)S(1)} collective-permute-done((bf16[128,2560]{1,0:T(8,128)(2,1)S(1)}, bf16[128,2560]{1,0:T(8,128)(2,1)S(1)}, u32[]{:S(2)}, u32[]{:S(2)}) %collective-permute-start.7) | collective-permute-done | bytes 655392 | tf_op jit(solution)/shard_map/ppermute | solution.py:22
  245.4 2.7 collective-permute-start.9
  248.0 13.7 %collective-permute-done.8 = bf16[128,2560]{1,0:T(8,128)(2,1)S(1)} collective-permute-done((bf16[128,2560]{1,0:T(8,128)(2,1)S(1)}, bf16[128,2560]{1,0:T(8,128)(2,1)S(1)}, u32[]{:S(2)}, u32[]{:S(2)}) %collective-permute-start.8) | collective-permute-done | bytes 655392 | tf_op jit(solution)/shard_map/ppermute | solution.py:22
  269.3 6.8 %fusion.60 = f32[512,800]{0,1:T(8,128)} fusion(bf16[2560,800]{1,0:T(8,128)(2,1)} %all-gather.12.cloned.1.call-done, bf16[1024,2560]{1,0:T(8,128)(2,1)} %constant_dynamic-update-slice_fusion.8, s32[]{:T(128)S(6)} %select_n.106), kind=kOutput, calls=%fused_computation.82 | convolution fusion | flops 2097152000 | bytes 8847364 | tf_op jit(solution)/shard_map/dot_general | solution.py:209
  276.1 11.9 %convolution_convert_fusion = bf16[512,2560]{1,0:T(8,128)(2,1)} fusion(bf16[800,2560]{0,1:T(8,128)(2,1)} %all-gather.14.cloned.1.call-done, f32[512,800]{0,1:T(8,128)} %fusion.60, bf16[2560,800]{1,0:T(8,128)(2,1)} %all-gather.10.cloned.1.call-done, bf16[1024,2560]{1,0:T(8,128)(2,1)} %constant_dynamic-update-slice_fusion.8, s32[]{:T(128)S(6)} %select_n.106), kind=kOutput, calls=%fused_computation.77 | convolution fusion | flops 4198072320 | bytes 16056324 | tf_op jit(solution)/shard_map/dot_general | solution.py:215
  288.0 32.6 %reduce-scatter.2.cloned.1.call-done = bf16[128,2560]{1,0:T(8,128)(2,1)} async-done(((bf16[512,2560]{1,0:T(8,128)(2,1)}), bf16[128,2560]{1,0:T(8,128)(2,1)}) %reduce-scatter.2.cloned.1.call-update) | async-done | bytes 655376 | tf_op jit(solution)/shard_map/reduce_scatter | solution.py:220
  (173 shorter events, 73.9 us)
Async XLA Ops:
  7.2 29.4 %copy-start = (bf16[768,1920]{1,0:T(8,128)(2,1)S(1)}, bf16[768,1920]{1,0:T(8,128)(2,1)}, u32[]{:S(2)}) copy-start(bf16[768,1920]{1,0:T(8,128)(2,1)} %param.29) | copy-start | bytes 8847364
  7.2 80.5 %all-gather.6.cloned.1.call-start = ((), (), s32[]{:S(2)}) async-start(), calls=%async_computation.1 | async-start | bytes 6488064 | tf_op jit(solution)/shard_map/all_gather | solution.py:158
  7.9 122.1 %all-gather.8.cloned.1.call-start = ((), (), s32[]{:S(2)}) async-start(), calls=%async_computation.2 | async-start | bytes 9732096 | tf_op jit(solution)/shard_map/all_gather | solution.py:157
  8.7 260.6 %all-gather.12.cloned.1.call-start = ((), (), s32[]{:S(2)}) async-start(), calls=%async_computation.4 | async-start | bytes 4730880 | tf_op jit(solution)/shard_map/all_gather | solution.py:211
  9.4 266.7 %all-gather.10.cloned.1.call-start = ((), (), s32[]{:S(2)}) async-start(), calls=%async_computation.3 | async-start | bytes 4730880 | tf_op jit(solution)/shard_map/all_gather | solution.py:206
  10.0 266.1 %all-gather.14.cloned.1.call-start = ((), (), s32[]{:S(2)}) async-start(), calls=%async_computation.5 | async-start | bytes 4730880 | tf_op jit(solution)/shard_map/all_gather | solution.py:217
  22.5 9.6 %copy-start.9 = (bf16[768]{0:T(1024)(128)(2,1)S(1)}, bf16[768]{0:T(1024)(128)(2,1)}, u32[]{:S(2)}) copy-start(bf16[768]{0:T(1024)(128)(2,1)} %param.28) | copy-start | bytes 4612
  22.5 14.0 %copy-start.7 = (bf16[128,288]{0,1:T(8,128)(2,1)}, bf16[128,288]{0,1:T(8,128)(2,1)S(1)}, u32[]{:S(2)}) copy-start(bf16[128,288]{0,1:T(8,128)(2,1)S(1)} %pad_maximum_fusion.1) | copy-start | bytes 221188
  22.5 9.5 %collective-permute-start = (bf16[128,288]{0,1:T(8,128)(2,1)S(1)}, bf16[128,288]{0,1:T(8,128)(2,1)}, u32[]{:S(2)}, u32[]{:S(2)}) collective-permute-start(bf16[128,288]{0,1:T(8,128)(2,1)S(1)} %pad_maximum_fusion.1), channel_id=1, source_target_pairs={{0,4},{1,5},{2,6},{3,7},{4,8},{5,9},{6,10},{7,11},{8,12},{9,13},{1... | collective-permute-start | bytes 221192 | tf_op jit(solution)/shard_map/ppermute | solution.py:41
  28.8 291.8 %reduce-scatter.2.cloned.1.call-start = ((), (), s32[]{:S(2)}) async-start(), calls=%async_computation.6 | async-start | bytes 3276800 | tf_op jit(solution)/shard_map/reduce_scatter | solution.py:220
  32.0 6.7 %collective-permute-start.1 = (bf16[128,288]{0,1:T(8,128)(2,1)}, bf16[128,288]{0,1:T(8,128)(2,1)}, u32[]{:S(2)}, u32[]{:S(2)}) collective-permute-start(bf16[128,288]{0,1:T(8,128)(2,1)} %collective-permute-done), channel_id=1, source_target_pairs={{0,4},{1,5},{2,6},{3,7},{4,8},{5,9},{6,10},{7,11},{8,12},{9,13},{1... | collective-permute-start | bytes 221192 | tf_op jit(solution)/shard_map/ppermute | solution.py:41
  38.8 5.7 %collective-permute-start.2 = (bf16[128,288]{0,1:T(8,128)(2,1)}, bf16[128,288]{0,1:T(8,128)(2,1)S(1)}, u32[]{:S(2)}, u32[]{:S(2)}) collective-permute-start(bf16[128,288]{0,1:T(8,128)(2,1)} %collective-permute-done.1), channel_id=1, source_target_pairs={{0,4},{1,5},{2,6},{3,7},{4,8},{5,9},{6,10},{7,11},{8,12},{9,13},{1... | collective-permute-start | bytes 221192 | tf_op jit(solution)/shard_map/ppermute | solution.py:41
  44.5 7.3 %collective-permute-start.3 = (bf16[128,288]{0,1:T(8,128)(2,1)S(1)}, bf16[128,288]{0,1:T(8,128)(2,1)S(1)}, u32[]{:S(2)}, u32[]{:S(2)}) collective-permute-start(bf16[128,288]{0,1:T(8,128)(2,1)S(1)} %collective-permute-done.2), channel_id=1, source_target_pairs={{0,4},{1,5},{2,6},{3,7},{4,8},{5,9},{6,10},{7,11},{8,12},{9,13},{1... | collective-permute-start | bytes 221192 | tf_op jit(solution)/shard_map/ppermute | solution.py:41
  51.8 11.4 %collective-permute-start.4 = (bf16[128,288]{0,1:T(8,128)(2,1)S(1)}, bf16[128,288]{0,1:T(8,128)(2,1)S(1)}, u32[]{:S(2)}, u32[]{:S(2)}) collective-permute-start(bf16[128,288]{0,1:T(8,128)(2,1)S(1)} %collective-permute-done.3), channel_id=1, source_target_pairs={{0,4},{1,5},{2,6},{3,7},{4,8},{5,9},{6,10},{7,11},{8,12},{9,13},{1... | collective-permute-start | bytes 221192 | tf_op jit(solution)/shard_map/ppermute | solution.py:41
  63.2 11.0 %copy-start.8 = (bf16[2560]{0:T(1024)(128)(2,1)S(1)}, bf16[2560]{0:T(1024)(128)(2,1)}, u32[]{:S(2)}) copy-start(bf16[2560]{0:T(1024)(128)(2,1)} %param.35) | copy-start | bytes 15364
  63.2 11.0 %collective-permute-start.5 = (bf16[128,288]{0,1:T(8,128)(2,1)S(1)}, bf16[128,288]{0,1:T(8,128)(2,1)S(1)}, u32[]{:S(2)}, u32[]{:S(2)}) collective-permute-start(bf16[128,288]{0,1:T(8,128)(2,1)S(1)} %collective-permute-done.4), channel_id=1, source_target_pairs={{0,4},{1,5},{2,6},{3,7},{4,8},{5,9},{6,10},{7,11},{8,12},{9,13},{1... | collective-permute-start | bytes 221192 | tf_op jit(solution)/shard_map/ppermute | solution.py:41
  74.2 6.6 %collective-permute-start.6 = (bf16[128,288]{0,1:T(8,128)(2,1)S(1)}, bf16[128,288]{0,1:T(8,128)(2,1)S(1)}, u32[]{:S(2)}, u32[]{:S(2)}) collective-permute-start(bf16[128,288]{0,1:T(8,128)(2,1)S(1)} %collective-permute-done.5), channel_id=1, source_target_pairs={{0,4},{1,5},{2,6},{3,7},{4,8},{5,9},{6,10},{7,11},{8,12},{9,13},{1... | collective-permute-start | bytes 221192 | tf_op jit(solution)/shard_map/ppermute | solution.py:41
  96.2 4.0 %copy-start.2 = (f32[512,2560]{1,0:T(8,128)S(1)}, f32[512,2560]{1,0:T(8,128)}, u32[]{:S(2)}) copy-start(f32[512,2560]{1,0:T(8,128)} %get-tuple-element.703) | copy-start | bytes 15728644 | tf_op jit(solution)/shard_map/while
  109.6 4.8 %copy-start.2 = (f32[512,2560]{1,0:T(8,128)S(1)}, f32[512,2560]{1,0:T(8,128)}, u32[]{:S(2)}) copy-start(f32[512,2560]{1,0:T(8,128)} %get-tuple-element.703) | copy-start | bytes 15728644 | tf_op jit(solution)/shard_map/while
  220.8 2.4 copy-start.5
  220.8 3.0 copy-start.4
  227.7 39.6 %copy-start.3 = (bf16[128,2560]{1,0:T(8,128)(2,1)}, bf16[128,2560]{1,0:T(8,128)(2,1)S(1)}, u32[]{:S(2)}) copy-start(bf16[128,2560]{1,0:T(8,128)(2,1)S(1)} %fusion.59) | copy-start | bytes 1966084
  228.1 1.3 copy-start.6
  228.2 17.2 %collective-permute-start.7 = (bf16[128,2560]{1,0:T(8,128)(2,1)S(1)}, bf16[128,2560]{1,0:T(8,128)(2,1)S(1)}, u32[]{:S(2)}, u32[]{:S(2)}) collective-permute-start(bf16[128,2560]{1,0:T(8,128)(2,1)S(1)} %fusion.70), channel_id=1, source_target_pairs={{0,32},{32,64},{64,96},{96,0},{1,33},{33,65},{65,97},{97,1},{2,34}... | collective-permute-start | bytes 1966088 | tf_op jit(solution)/shard_map/ppermute | solution.py:22
  245.4 16.4 %collective-permute-start.8 = (bf16[128,2560]{1,0:T(8,128)(2,1)S(1)}, bf16[128,2560]{1,0:T(8,128)(2,1)S(1)}, u32[]{:S(2)}, u32[]{:S(2)}) collective-permute-start(bf16[128,2560]{1,0:T(8,128)(2,1)S(1)} %collective-permute-done.7), channel_id=1, source_target_pairs={{0,32},{32,64},{64,96},{96,0},{1,33},{33,65},{65,97},{97,1},{2,34}... | collective-permute-start | bytes 1966088 | tf_op jit(solution)/shard_map/ppermute | solution.py:22
  245.4 19.3 %collective-permute-start.9 = (bf16[128,2560]{1,0:T(8,128)(2,1)}, bf16[128,2560]{1,0:T(8,128)(2,1)S(1)}, u32[]{:S(2)}, u32[]{:S(2)}) collective-permute-start(bf16[128,2560]{1,0:T(8,128)(2,1)} %copy-done.6), channel_id=1, source_target_pairs={{0,96},{32,0},{64,32},{96,64},{1,97},{33,1},{65,33},{97,65},{2,98}... | collective-permute-start | bytes 1966088 | tf_op jit(solution)/shard_map/ppermute | solution.py:24
  276.1 46.8 %copy-start.1 = (bf16[768,1920]{1,0:T(8,128)(2,1)S(1)}, bf16[768,1920]{1,0:T(8,128)(2,1)}, u32[]{:S(2)}) copy-start(bf16[768,1920]{1,0:T(8,128)(2,1)} %param.29) | copy-start | bytes 8847364
Sparse Core Ops, SparseCore 0:
  10.3 56.2 all-gather.5
  68.7 61.1 all-gather.7
  132.3 46.1 all-gather.11
  180.7 45.8 all-gather.9
  228.7 45.8 all-gather.13
  288.1 32.4 reduce-scatter.1
